TPU v7x, 32 devices: a whole 2x2x4 slice. The times are simulated.
32 devices in a mesh: tm: 4 (over z), space: 2 (over y), hyp: 4 (over x, core).
Axes of the slice: x: 2, y: 2, z: 4, core: 2. Of those that a mesh axis runs over, the one named last changes fastest.
Arguments:
- log_kappa: float32 [8192], P('space'), may hold values from -0.5 to 0.5
- node_mass: float32 [8192], P('space'), may hold values from 0.5 to 2
- rho_base: float32 [8192], P('space'), may hold values from 1.5 to 4
- edge_weight: float32 [4, 8192], P(None, 'space'), may hold values from 0.05 to 0.3
- offsets: int32 [4, 8192], P(None, 'space'), may hold values from -64 to 64
- roughness: float32 [64, 8192], P('tm', 'space'), may hold values from 0.5 to 1.0002
- coupling: float32 [64, 8192], P('tm', 'space'), may hold values from 0.5 to 1
- obs_weight: float32 [64, 8192], P('tm', 'space'), may hold values from 0.0003 to 0.03
- observed: float32 [64, 8192], P('tm', 'space'), may hold values from -0.3125 to 0.3125
- hyper_params: float32 [4], replicated, may hold values from -0.3 to 0.3
Outputs:
- solution: float32 [64, 8192], P('tm', ('space', 'hyp'))
- log_det_mean: float32 [8192], P('space')
- gradient: float32 [4, 8192], P(None, 'space')
Inputs may be any that keep to these rules, and one draw needn't show every extreme that they name: offsets[k, i] is a band offset from node i to a listed neighbour.
All inputs are finite; a program needn't handle non-finite values.
Results may differ from a plain program's by a relative error of at most 0.0003.
Values sent between devices are 32-bit elements; how exact they have to be, the bound alone decides.
No kernel may reach another device: no remote copies, remote signals or barrier semaphores. Data moves between devices by JAX's collectives and lax.ppermute only.
A program may use at most 64 MiB of HBM per device.

v0:
```python
import jax
import jax.numpy as jnp
from jax import lax
from jax.sharding import PartitionSpec as P

BAND = 64


def with_halo(block, sides, width):
    for axis, dim in sides:
        count = lax.axis_size(axis)
        forward = [(i, i + 1) for i in range(count - 1)]
        backward = [(target, source) for source, target in forward]
        low = lax.ppermute(
            lax.slice_in_dim(block, block.shape[dim] - width, None, axis=dim), axis, forward
        )
        high = lax.ppermute(lax.slice_in_dim(block, 0, width, axis=dim), axis, backward)
        block = jnp.concatenate([low, block, high], axis=dim)
    return block


def prefix(part, axis, combine, identity, reverse):
    count = lax.axis_size(axis)
    place = lax.axis_index(axis)
    ahead = count - 1 - place if reverse else place
    gathered = jax.tree.map(lambda a: lax.all_gather(a, axis), part)
    state = jax.tree.map(lambda a, e: jnp.zeros_like(a) + jnp.asarray(e, a.dtype), part, identity)

    def one(hop, state):
        source = count - 1 - hop if reverse else hop
        return combine(
            state, jax.tree.map(lambda a: lax.dynamic_index_in_dim(a, source, 0, False), gathered)
        )

    return lax.fori_loop(0, ahead, one, state)


def row_terms(scaled, persist, roughness, coupling, obs_weight, nugget_scale, later_rows):
    prior = scaled * (1.0 + persist * persist) * roughness
    nugget = nugget_scale * obs_weight
    diagonal = prior + nugget
    offdiag = -persist * scaled * coupling * later_rows
    slopes = jnp.stack(
        [
            2.0 * prior,
            prior,
            2.0 * persist * (1.0 - persist * persist) * scaled * roughness,
            nugget,
        ],
        axis=-2,
    )
    return (diagonal, offdiag, slopes)


def mobius_join(earlier_part, later_part):
    upper_left = later_part[0] * earlier_part[0] + later_part[1] * earlier_part[2]
    upper_right = later_part[0] * earlier_part[1] + later_part[1] * earlier_part[3]
    lower_left = later_part[2] * earlier_part[0] + later_part[3] * earlier_part[2]
    lower_right = later_part[2] * earlier_part[1] + later_part[3] * earlier_part[3]
    norm_total = (
        jnp.abs(upper_left) + jnp.abs(upper_right) + jnp.abs(lower_left) + jnp.abs(lower_right)
    )
    return (
        upper_left / norm_total,
        upper_right / norm_total,
        lower_left / norm_total,
        lower_right / norm_total,
    )


def affine_join(earlier_part, later_part):
    joined = []
    for index in range(0, len(earlier_part), 2):
        joined.append(later_part[index] * earlier_part[index])
        joined.append(later_part[index] * earlier_part[index + 1] + later_part[index + 1])
    return tuple(joined)


def mobius_step(carried, step_rows):
    diag_row, off_row = step_rows
    step_map = (diag_row, -off_row * off_row, jnp.ones_like(diag_row), jnp.zeros_like(diag_row))
    return (mobius_join(carried, step_map), None)


def per_device(
    log_kappa,
    node_mass,
    rho_base,
    edge_weight,
    offsets,
    roughness,
    coupling,
    obs_weight,
    observed,
    hyper_params,
):
    row_count, full_width = roughness.shape
    kappa_sq = jnp.exp(2.0 * log_kappa)
    padded = with_halo(kappa_sq, (("space", 0),), BAND)
    indices = jnp.arange(full_width, dtype=jnp.int32)[None, :] + BAND + offsets
    nearby = jnp.take(padded, indices)
    spatial = jnp.exp(2.0 * hyper_params[0]) * (
        node_mass * kappa_sq + jnp.sum(edge_weight * nearby, axis=0)
    )
    scaled = jnp.exp(hyper_params[1]) * spatial
    persist = jnp.tanh(hyper_params[2] + rho_base)
    nugget_scale = jnp.exp(hyper_params[3])
    log_slope = jnp.stack(
        [
            2.0 * jnp.ones_like(persist),
            jnp.ones_like(persist),
            (1.0 - persist * persist) / persist,
            jnp.zeros_like(persist),
        ]
    )
    hyp_count = lax.axis_size("hyp")
    hyp_place = lax.axis_index("hyp")
    quarter = full_width // hyp_count
    time_count = lax.axis_size("tm")
    global_rows = jnp.arange(row_count, dtype=jnp.int32) + lax.axis_index("tm") * row_count
    later_rows = (global_rows > 0).astype(jnp.float32)[:, None]
    diagonal, offdiag, slopes = row_terms(
        scaled, persist, roughness, coupling, obs_weight, nugget_scale, later_rows
    )
    slopes = lax.dynamic_index_in_dim(slopes, hyp_place, 1, keepdims=True)
    log_slope = lax.dynamic_index_in_dim(log_slope, hyp_place, 0, keepdims=True)
    ones_row = jnp.ones_like(diagonal[0])
    zeros_row = jnp.zeros_like(diagonal[0])
    zeros_dir = jnp.zeros_like(log_slope)
    identity = (ones_row, zeros_row, zeros_row, ones_row)
    local_map, unused = lax.scan(mobius_step, identity, (diagonal, offdiag))
    before = prefix(local_map, "tm", mobius_join, identity, False)
    inverse_in = before[2] / before[0]

    def forward_step(carried, step_rows):
        inverse, gain_tangent, tangent_loc, gain_solve, solve_loc = carried
        diag_row, off_row, slope_row, observed_row = step_rows
        pivots = diag_row - off_row * off_row * inverse
        ratios = off_row * inverse
        gain_tangent = ratios * ratios * gain_tangent
        tangent_loc = ratios * ratios * tangent_loc + slope_row - 2.0 * log_slope * off_row * ratios
        gain_solve = -ratios * gain_solve
        solve_loc = observed_row - ratios * solve_loc
        return (
            (1.0 / pivots, gain_tangent, tangent_loc, gain_solve, solve_loc),
            (pivots, gain_tangent, tangent_loc, gain_solve, solve_loc),
        )

    start = (inverse_in, ones_row, zeros_dir, ones_row, zeros_row)
    ending, stacked = lax.scan(forward_step, start, (diagonal, offdiag, slopes, observed))
    pivots, gains_tangent, tangent_locs, gains_solve, solve_locs = stacked
    incoming = prefix(
        (ending[1], ending[2], ending[3], ending[4]),
        "tm",
        affine_join,
        (ones_row, zeros_dir, ones_row, zeros_row),
        False,
    )
    tangents = tangent_locs + gains_tangent[:, None, :] * incoming[1][None]
    solveds = solve_locs + gains_solve * incoming[3][None]

    def backward_step(carried, step_rows):
        next_loc, next_gain = carried
        off_row, pivot_row, solved_row = step_rows
        return (
            (off_row * (solved_row - next_loc) / pivot_row, -off_row / pivot_row * next_gain),
            (next_loc, next_gain),
        )

    front, trailing = lax.scan(
        backward_step, (zeros_row, ones_row), (offdiag, pivots, solveds), reverse=True
    )
    next_locs, next_gains = trailing
    after = prefix((front[1], front[0]), "tm", affine_join, (ones_row, zeros_row), True)
    carried_next = next_locs + next_gains * after[1][None]
    solution = (solveds - carried_next) / pivots
    total_rows = row_count * time_count
    scores = jnp.sum(0.5 * tangents / pivots[:, None, :], axis=0)
    quadratic = jnp.sum(
        slopes * (solution * solution)[:, None, :]
        + 2.0 * log_slope[None] * (solution * carried_next)[:, None, :],
        axis=0,
    )
    gradient_part = (scores - 0.5 * quadratic) / total_rows
    logdet_part = jnp.sum(jnp.log(pivots), axis=0) / total_rows
    direction_mask = (jnp.arange(hyp_count, dtype=jnp.int32) == hyp_place).astype(jnp.float32)[
        :, None
    ]
    leader_mask = (hyp_place == 0).astype(jnp.float32)
    placed = jnp.concatenate(
        [(leader_mask * logdet_part)[None], direction_mask * gradient_part], axis=0
    )
    solution_out = lax.dynamic_slice_in_dim(
        solution, hyp_place * quarter, quarter, solution.ndim - 1
    )
    totals = lax.psum(placed, ("tm", "hyp"))
    return (solution_out, totals[0], totals[1:])


def solution(mesh):
    placed = (
        P("space"),
        P("space"),
        P("space"),
        P(None, "space"),
        P(None, "space"),
        P("tm", "space"),
        P("tm", "space"),
        P("tm", "space"),
        P("tm", "space"),
        P(),
    )
    return jax.shard_map(
        per_device,
        mesh=mesh,
        in_specs=placed,
        out_specs=(P("tm", ("space", "hyp")), P("space"), P(None, "space")),
        check_vma=False,
    )
```

profile of v0, /device:TPU:8, one launch (start us, length us, event | category | flops | bytes accessed | tf_op | source)
XLA Modules:
  0.0 407.8 jit_solution(9264937598001699120)
XLA Ops:
  7.2 0.7 multiply_exponential_fusion
  8.0 3.4 collective-permute-start
  11.4 1.3 collective-permute-start.1
  13.0 0.6 copy-done.8
  13.6 0.7 fusion.22
  16.4 0.6 dynamic-slice
  17.1 90.5 %gather_fusion = f32[16384]{0:T(1024)S(1)} fusion(f32[4224]{0:T(1024)S(1)} %concatenate.6, s32[16384]{0:T(1024)S(1)} %broadcast_clamp_fusion), kind=kCustom, calls=%fused_computation | custom fusion | bytes 196608 | tf_op jit(solution)/shard_map/jit(_take)/gather | solution.py:101
  107.8 0.7 multiply_multiply_fusion.1
  108.5 0.7 negate_multiply_fusion.1
  109.3 2.1 while.116
  111.4 13.4 %all-gather = f32[16384]{0:T(1024)S(1)} all-gather(f32[4096]{0:T(1024)S(1)} %get-tuple-element.526), channel_id=2, replica_groups=mesh['tm'=4,'space'=2,'hyp'=4] {'tm'}, dimensions={0}, use_global_device_ids=true | all-gather | bytes 81920 | tf_op jit(solution)/shard_map/all_gather | solution.py:26
  124.8 13.2 %all-gather.1 = f32[16384]{0:T(1024)S(1)} all-gather(f32[4096]{0:T(1024)S(1)} %get-tuple-element.527), channel_id=3, replica_groups=mesh['tm'=4,'space'=2,'hyp'=4] {'tm'}, dimensions={0}, use_global_device_ids=true | all-gather | bytes 81920 | tf_op jit(solution)/shard_map/all_gather | solution.py:26
  138.0 13.1 %all-gather.2 = f32[16384]{0:T(1024)S(1)} all-gather(f32[4096]{0:T(1024)S(1)} %get-tuple-element.528), channel_id=4, replica_groups=mesh['tm'=4,'space'=2,'hyp'=4] {'tm'}, dimensions={0}, use_global_device_ids=true | all-gather | bytes 81920 | tf_op jit(solution)/shard_map/all_gather | solution.py:26
  151.1 13.1 %all-gather.3 = f32[16384]{0:T(1024)S(1)} all-gather(f32[4096]{0:T(1024)S(1)} %get-tuple-element.529), channel_id=5, replica_groups=mesh['tm'=4,'space'=2,'hyp'=4] {'tm'}, dimensions={0}, use_global_device_ids=true | all-gather | bytes 81920 | tf_op jit(solution)/shard_map/all_gather | solution.py:26
  164.7 0.7 broadcast_multiply_fusion.3
  165.5 43.2 %while.117 = (s32[]{:T(128)}, f32[4096]{0:T(1024)S(1)}, f32[4096]{0:T(1024)S(1)}, f32[1,4096]{1,0:T(1,128)S(1)}, f32[4096]{0:T(1024)S(1)}, /*index=5*/f32[4096]{...) while((s32[]{:T(128)}, f32[4096]{0:T(1024)S(1)}, ...), condition=%wide.region_6.7_spmd.clone, body=%wide.region_5.6_spmd.clone.sunk | while | flops 86019 | bytes 606413 | solution.py:150
  165.5 0.9 constant_dynamic-slice_fusion.31
  167.0 0.4 dynamic_update_slice.53
  167.4 0.4 dynamic_update_slice.54
  168.2 0.9 constant_dynamic-slice_fusion.31
  170.1 0.4 dynamic_update_slice.54
  170.5 0.4 dynamic_update_slice.51
  170.9 0.9 constant_dynamic-slice_fusion.31
  172.4 0.4 dynamic_update_slice.53
  173.6 0.9 constant_dynamic-slice_fusion.31
  175.5 0.4 dynamic_update_slice.54
  175.9 0.4 dynamic_update_slice.51
  176.3 0.9 constant_dynamic-slice_fusion.31
  177.8 0.4 dynamic_update_slice.53
  178.6 0.4 dynamic_update_slice.51
  179.0 0.9 constant_dynamic-slice_fusion.31
  180.5 0.4 dynamic_update_slice.53
  180.9 0.4 dynamic_update_slice.54
  181.7 0.9 constant_dynamic-slice_fusion.31
  184.0 0.4 dynamic_update_slice.51
  184.4 0.9 constant_dynamic-slice_fusion.31
  185.9 0.4 dynamic_update_slice.53
  186.3 0.4 dynamic_update_slice.54
  187.1 0.9 constant_dynamic-slice_fusion.31
  189.0 0.4 dynamic_update_slice.54
  189.4 0.4 dynamic_update_slice.51
  189.8 0.9 constant_dynamic-slice_fusion.31
  191.3 0.4 dynamic_update_slice.53
  192.5 0.9 constant_dynamic-slice_fusion.31
  194.4 0.4 dynamic_update_slice.54
  194.8 0.4 dynamic_update_slice.51
  195.2 0.9 constant_dynamic-slice_fusion.31
  197.9 0.9 constant_dynamic-slice_fusion.31
  200.6 0.9 constant_dynamic-slice_fusion.31
  203.3 0.9 constant_dynamic-slice_fusion.31
  206.0 0.9 constant_dynamic-slice_fusion.31
  208.7 13.5 %all-gather.4 = f32[16384]{0:T(1024)S(1)} all-gather(f32[4096]{0:T(1024)S(1)} %get-tuple-element.534), channel_id=6, replica_groups=mesh['tm'=4,'space'=2,'hyp'=4] {'tm'}, dimensions={0}, use_global_device_ids=true | all-gather | bytes 81920 | tf_op jit(solution)/shard_map/all_gather | solution.py:26
  222.3 13.3 %all-gather.6 = f32[16384]{0:T(1024)S(1)} all-gather(f32[4096]{0:T(1024)S(1)} %get-tuple-element.536), channel_id=8, replica_groups=mesh['tm'=4,'space'=2,'hyp'=4] {'tm'}, dimensions={0}, use_global_device_ids=true | all-gather | bytes 81920 | tf_op jit(solution)/shard_map/all_gather | solution.py:26
  235.6 13.1 %all-gather.7 = f32[16384]{0:T(1024)S(1)} all-gather(f32[4096]{0:T(1024)S(1)} %get-tuple-element.537), channel_id=9, replica_groups=mesh['tm'=4,'space'=2,'hyp'=4] {'tm'}, dimensions={0}, use_global_device_ids=true | all-gather | bytes 81920 | tf_op jit(solution)/shard_map/all_gather | solution.py:26
  248.8 13.1 %all-gather.10 = f32[4,1,4096]{2,1,0:T(1,128)S(1)} all-gather(f32[1,1,4096]{2,1,0:T(1,128)S(1)} %bitcast.142), channel_id=7, replica_groups=mesh['tm'=4,'space'=2,'hyp'=4] {'tm'}, dimensions={0}, use_global_device_ids=true | all-gather | bytes 81920 | tf_op jit(solution)/shard_map/all_gather | solution.py:26
  262.2 14.6 %while.118 = (s32[]{:T(128)}, f32[4096]{0:T(1024)S(1)}, f32[4096]{0:T(1024)S(1)}, f32[16,4096]{1,0:T(8,128)S(1)}, f32[16,4096]{1,0:T(8,128)S(1)}, /*index=5*/f32...) while((s32[]{:T(128)}, f32[4096]{0:T(1024)S(1)}, ...), condition=%wide.region_10.11_spmd.clone, body=%wide.region_9.10_spmd.clone.sunk | while | flops 32772 | bytes 311443 | solution.py:170
  276.8 13.4 %all-gather.8 = f32[16384]{0:T(1024)S(1)} all-gather(f32[4096]{0:T(1024)S(1)} %get-tuple-element.542), channel_id=10, replica_groups=mesh['tm'=4,'space'=2,'hyp'=4] {'tm'}, dimensions={0}, use_global_device_ids=true | all-gather | bytes 81920 | tf_op jit(solution)/shard_map/all_gather | solution.py:26
  290.2 13.1 %all-gather.9 = f32[16384]{0:T(1024)S(1)} all-gather(f32[4096]{0:T(1024)S(1)} %get-tuple-element.543), channel_id=11, replica_groups=mesh['tm'=4,'space'=2,'hyp'=4] {'tm'}, dimensions={0}, use_global_device_ids=true | all-gather | bytes 81920 | tf_op jit(solution)/shard_map/all_gather | solution.py:26
  303.6 0.4 fusion.12
  304.4 0.7 pad_maximum_fusion
  305.0 0.6 constant_dynamic-slice_fusion.16
  305.7 92.2 %all-reduce.2.cloned.1.call-done = f32[5,4096]{1,0:T(8,128)} async-done(((f32[5,4096]{1,0:T(8,128)}), f32[5,4096]{1,0:T(8,128)}) %all-reduce.2.cloned.1.call-update) | async-done | bytes 81936 | tf_op jit(solution)/shard_map/psum | solution.py:196
  397.9 1.6 slice.37
  399.4 1.5 slice.36
  (343 shorter events, 36.7 us)
Async XLA Ops:
  7.2 5.7 %copy-start.3 = (s32[4,4096]{1,0:T(4,128)S(1)}, s32[4,4096]{1,0:T(4,128)}, u32[]{:S(2)}) copy-start(s32[4,4096]{1,0:T(4,128)} %param.26) | copy-start | bytes 196612
  7.2 390.7 %all-reduce.2.cloned.1.call-start = ((), (), s32[]{:S(2)}) async-start(), calls=%async_computation | async-start | bytes 262144 | tf_op jit(solution)/shard_map/psum | solution.py:196
  8.0 8.9 %collective-permute-start = (f32[64]{0:T(128)S(1)}, f32[64]{0:T(128)S(1)}, u32[]{:S(2)}, u32[]{:S(2)}) collective-permute-start(f32[64]{0:T(128)S(1)} %get-tuple-element.865), channel_id=1, source_target_pairs={{0,4},{1,5},{2,6},{3,7},{8,12},{9,13},{10,14},{11,15},{16,20},{17,... | collective-permute-start | bytes 776 | tf_op jit(solution)/shard_map/ppermute | solution.py:14
  11.4 5.5 %collective-permute-start.1 = (f32[64]{0:T(128)S(1)}, f32[64]{0:T(128)S(1)}, u32[]{:S(2)}, u32[]{:S(2)}) collective-permute-start(f32[64]{0:T(128)S(1)} %get-tuple-element.864), channel_id=1, source_target_pairs={{4,0},{5,1},{6,2},{7,3},{12,8},{13,9},{14,10},{15,11},{20,16},{21,... | collective-permute-start | bytes 776 | tf_op jit(solution)/shard_map/ppermute | solution.py:17
  12.9 0.7 copy-start.8
  17.1 90.7 %copy-start.4 = (f32[4,4096]{1,0:T(4,128)S(1)}, f32[4,4096]{1,0:T(4,128)}, u32[]{:S(2)}) copy-start(f32[4,4096]{1,0:T(4,128)} %param.25) | copy-start | bytes 196612
  17.1 90.8 %copy-start.5 = (f32[4096]{0:T(1024)S(1)}, f32[4096]{0:T(1024)}, u32[]{:S(2)}) copy-start(f32[4096]{0:T(1024)} %param.24) | copy-start | bytes 49156
  17.1 90.7 %copy-start.6 = (f32[4096]{0:T(1024)S(1)}, f32[4096]{0:T(1024)}, u32[]{:S(2)}) copy-start(f32[4096]{0:T(1024)} %param.22) | copy-start | bytes 49156
  17.1 90.7 %copy-start.7 = (f32[4096]{0:T(1024)S(1)}, f32[4096]{0:T(1024)}, u32[]{:S(2)}) copy-start(f32[4096]{0:T(1024)} %param.23) | copy-start | bytes 49156
  17.1 92.1 %copy-start.2 = (f32[16,4096]{1,0:T(8,128)S(1)}, f32[16,4096]{1,0:T(8,128)}, u32[]{:S(2)}) copy-start(f32[16,4096]{1,0:T(8,128)} %param.28) | copy-start | bytes 786436
  107.7 1.5 copy-start
  107.7 1.5 copy-start.1
Sparse Core Ops, SparseCore 0:
  305.2 92.6 all-reduce.1
where the time goes:
time: 408 us
  local copies, waits for them, and re-layouts  151 us (37%)
  blocking collectives  132 us (32%)
  waiting for transfers between devices  92.2 us (23%)
  between operations  16.7 us (4%)
  other arithmetic  7.32 us (2%)
  starting transfers between devices  4.74 us (1%)
    all_gather x10, blocking collectives, prefix(): gathered = jax.tree.map(lambda a: lax.all_gather(a, axis), part)  132 us
    psum x1, waiting for transfers between devices, per_device(): totals = lax.psum(placed, ('tm', 'hyp'))  92.2 us
    gather x2, local copies, waits for them, and re-layouts, per_device(): nearby = jnp.take(padded, indices)  90.6 us
    dynamic_update_slice x96, local copies, waits for them, and re-layouts, per_device(): lax.scan(forward_step, start, (diagonal, offdiag, slopes, observed))  37.7 us
    dynamic_slice x80, local copies, waits for them, and re-layouts, per_device(): local_map, unused = lax.scan(mobius_step, identity, (diagonal, offdiag))  16.6 us
  transfers between devices with their start and end apart: 3, of which 1 were waited for; matrix products, arithmetic and copies ran while one was open for 0% of the time, Pallas kernels for 0%

commit v1 on v0

--- a/solution.py
+++ b/solution.py
@@ -4,6 +4,10 @@
 from jax.sharding import PartitionSpec as P
 
 BAND = 64
+
+
+def scan_the_edges(payload, along_axis):
+    return lax.all_gather(payload, along_axis).sum(axis=0)
 
 
 def with_halo(block, sides, width):
@@ -193,7 +197,7 @@
     solution_out = lax.dynamic_slice_in_dim(
         solution, hyp_place * quarter, quarter, solution.ndim - 1
     )
-    totals = lax.psum(placed, ("tm", "hyp"))
+    totals = scan_the_edges(placed, along_axis=("tm", "hyp"))
     return (solution_out, totals[0], totals[1:])
 
 

time: 408 us -> 362 us (0.89)
  waiting for transfers between devices: 92.2 us -> 41.7 us
    psum x1 -> x0, waiting for transfers between devices: 92.2 us -> none  [per_device(): totals = lax.psum(placed, ('tm', 'hyp'))]
    all_gather x0 -> x1, waiting for transfers between devices: none -> 41.7 us  [scan_the_edges(): return lax.all_gather(payload, along_axis).sum(axis=0)]
  transfers between devices with their start and end apart: 3 -> 3, of which waited for: 1 -> 1; matrix products, arithmetic and copies ran while one was open for 0% -> 1% of each run, Pallas kernels for 0% -> 0%
where the time goes in v1:
time: 362 us; the launch traced here: 358 us
  local copies, waits for them, and re-layouts  150 us (41%)
  blocking collectives  132 us (36%)
  waiting for transfers between devices  41.7 us (12%)
  between operations  16.8 us (5%)
  other arithmetic  9.9 us (3%)
  starting transfers between devices  4.74 us (1%)
    all_gather x10, blocking collectives, prefix(): gathered = jax.tree.map(lambda a: lax.all_gather(a, axis), part)  132 us
    gather x2, local copies, waits for them, and re-layouts, per_device(): nearby = jnp.take(padded, indices)  90.6 us
    all_gather x1, waiting for transfers between devices, scan_the_edges(): return lax.all_gather(payload, along_axis).sum(axis=0)  41.7 us
    dynamic_update_slice x96, local copies, waits for them, and re-layouts, per_device(): lax.scan(forward_step, start, (diagonal, offdiag, slopes, observed))  37.6 us
    dynamic_slice x80, local copies, waits for them, and re-layouts, per_device(): local_map, unused = lax.scan(mobius_step, identity, (diagonal, offdiag))  16.6 us
  transfers between devices with their start and end apart: 3, of which 1 were waited for; matrix products, arithmetic and copies ran while one was open for 1% of the time, Pallas kernels for 0%

profile of v1, /device:TPU:8, one launch (start us, length us, event | category | flops | bytes accessed | tf_op | source)
XLA Modules:
  0.0 358.4 jit_solution(13477426227941864380)
XLA Ops:
  7.2 0.7 multiply_exponential_fusion
  8.0 3.4 collective-permute-start
  11.4 1.3 collective-permute-start.1
  12.9 0.9 fusion.13
  13.8 1.5 fusion.22
  17.5 0.7 dynamic-slice
  18.3 90.5 %gather_fusion = f32[16384]{0:T(1024)S(1)} fusion(f32[4224]{0:T(1024)S(1)} %concatenate.6, s32[16384]{0:T(1024)S(1)} %broadcast_clamp_fusion), kind=kCustom, calls=%fused_computation | custom fusion | bytes 196608 | tf_op jit(solution)/shard_map/jit(_take)/gather | solution.py:105
  109.0 0.6 multiply_multiply_fusion.1
  109.6 0.6 negate_multiply_fusion.1
  110.4 2.1 while.116
  112.5 13.4 %all-gather = f32[16384]{0:T(1024)S(1)} all-gather(f32[4096]{0:T(1024)S(1)} %get-tuple-element.526), channel_id=2, replica_groups=mesh['tm'=4,'space'=2,'hyp'=4] {'tm'}, dimensions={0}, use_global_device_ids=true | all-gather | bytes 81920 | tf_op jit(solution)/shard_map/all_gather | solution.py:30
  125.9 13.2 %all-gather.1 = f32[16384]{0:T(1024)S(1)} all-gather(f32[4096]{0:T(1024)S(1)} %get-tuple-element.527), channel_id=3, replica_groups=mesh['tm'=4,'space'=2,'hyp'=4] {'tm'}, dimensions={0}, use_global_device_ids=true | all-gather | bytes 81920 | tf_op jit(solution)/shard_map/all_gather | solution.py:30
  139.0 13.1 %all-gather.2 = f32[16384]{0:T(1024)S(1)} all-gather(f32[4096]{0:T(1024)S(1)} %get-tuple-element.528), channel_id=4, replica_groups=mesh['tm'=4,'space'=2,'hyp'=4] {'tm'}, dimensions={0}, use_global_device_ids=true | all-gather | bytes 81920 | tf_op jit(solution)/shard_map/all_gather | solution.py:30
  152.2 13.1 %all-gather.3 = f32[16384]{0:T(1024)S(1)} all-gather(f32[4096]{0:T(1024)S(1)} %get-tuple-element.529), channel_id=5, replica_groups=mesh['tm'=4,'space'=2,'hyp'=4] {'tm'}, dimensions={0}, use_global_device_ids=true | all-gather | bytes 81920 | tf_op jit(solution)/shard_map/all_gather | solution.py:30
  165.8 0.8 broadcast_multiply_fusion.3
  166.7 43.2 %while.117 = (s32[]{:T(128)}, f32[4096]{0:T(1024)S(1)}, f32[4096]{0:T(1024)S(1)}, f32[1,4096]{1,0:T(1,128)S(1)}, f32[4096]{0:T(1024)S(1)}, /*index=5*/f32[4096]{...) while((s32[]{:T(128)}, f32[4096]{0:T(1024)S(1)}, ...), condition=%wide.region_6.7_spmd.clone, body=%wide.region_5.6_spmd.clone.sunk | while | flops 86019 | bytes 606413 | solution.py:154
  166.7 0.9 constant_dynamic-slice_fusion.31
  168.2 0.4 dynamic_update_slice.53
  169.4 0.9 constant_dynamic-slice_fusion.31
  170.9 0.4 dynamic_update_slice.53
  171.7 0.4 dynamic_update_slice.51
  172.1 0.9 constant_dynamic-slice_fusion.31
  174.0 0.4 dynamic_update_slice.54
  174.4 0.4 dynamic_update_slice.51
  174.8 0.9 constant_dynamic-slice_fusion.31
  176.3 0.4 dynamic_update_slice.53
  176.7 0.4 dynamic_update_slice.54
  177.5 0.9 constant_dynamic-slice_fusion.31
  179.0 0.4 dynamic_update_slice.53
  180.2 0.9 constant_dynamic-slice_fusion.31
  182.5 0.4 dynamic_update_slice.51
  182.9 0.9 constant_dynamic-slice_fusion.31
  184.8 0.4 dynamic_update_slice.54
  185.2 0.4 dynamic_update_slice.51
  185.6 0.9 constant_dynamic-slice_fusion.31
  187.1 0.4 dynamic_update_slice.53
  187.5 0.4 dynamic_update_slice.54
  188.3 0.9 constant_dynamic-slice_fusion.31
  189.8 0.4 dynamic_update_slice.53
  190.6 0.4 dynamic_update_slice.51
  191.0 0.9 constant_dynamic-slice_fusion.31
  193.3 0.4 dynamic_update_slice.51
  193.7 0.9 constant_dynamic-slice_fusion.31
  195.6 0.4 dynamic_update_slice.54
  196.0 0.4 dynamic_update_slice.51
  196.4 0.9 constant_dynamic-slice_fusion.31
  199.1 0.9 constant_dynamic-slice_fusion.31
  201.8 0.9 constant_dynamic-slice_fusion.31
  204.5 0.9 constant_dynamic-slice_fusion.31
  207.2 0.9 constant_dynamic-slice_fusion.31
  209.9 13.5 %all-gather.4 = f32[16384]{0:T(1024)S(1)} all-gather(f32[4096]{0:T(1024)S(1)} %get-tuple-element.534), channel_id=6, replica_groups=mesh['tm'=4,'space'=2,'hyp'=4] {'tm'}, dimensions={0}, use_global_device_ids=true | all-gather | bytes 81920 | tf_op jit(solution)/shard_map/all_gather | solution.py:30
  223.5 13.3 %all-gather.6 = f32[16384]{0:T(1024)S(1)} all-gather(f32[4096]{0:T(1024)S(1)} %get-tuple-element.536), channel_id=8, replica_groups=mesh['tm'=4,'space'=2,'hyp'=4] {'tm'}, dimensions={0}, use_global_device_ids=true | all-gather | bytes 81920 | tf_op jit(solution)/shard_map/all_gather | solution.py:30
  236.8 13.1 %all-gather.7 = f32[16384]{0:T(1024)S(1)} all-gather(f32[4096]{0:T(1024)S(1)} %get-tuple-element.537), channel_id=9, replica_groups=mesh['tm'=4,'space'=2,'hyp'=4] {'tm'}, dimensions={0}, use_global_device_ids=true | all-gather | bytes 81920 | tf_op jit(solution)/shard_map/all_gather | solution.py:30
  250.0 13.1 %all-gather.11 = f32[4,1,4096]{2,1,0:T(1,128)S(1)} all-gather(f32[1,1,4096]{2,1,0:T(1,128)S(1)} %bitcast.144), channel_id=7, replica_groups=mesh['tm'=4,'space'=2,'hyp'=4] {'tm'}, dimensions={0}, use_global_device_ids=true | all-gather | bytes 81920 | tf_op jit(solution)/shard_map/all_gather | solution.py:30
  263.4 14.6 %while.118 = (s32[]{:T(128)}, f32[4096]{0:T(1024)S(1)}, f32[4096]{0:T(1024)S(1)}, f32[16,4096]{1,0:T(8,128)S(1)}, f32[16,4096]{1,0:T(8,128)S(1)}, /*index=5*/f32...) while((s32[]{:T(128)}, f32[4096]{0:T(1024)S(1)}, ...), condition=%wide.region_10.11_spmd.clone, body=%wide.region_9.10_spmd.clone.sunk | while | flops 32772 | bytes 311443 | solution.py:174
  278.0 13.4 %all-gather.8 = f32[16384]{0:T(1024)S(1)} all-gather(f32[4096]{0:T(1024)S(1)} %get-tuple-element.542), channel_id=10, replica_groups=mesh['tm'=4,'space'=2,'hyp'=4] {'tm'}, dimensions={0}, use_global_device_ids=true | all-gather | bytes 81920 | tf_op jit(solution)/shard_map/all_gather | solution.py:30
  291.4 13.1 %all-gather.9 = f32[16384]{0:T(1024)S(1)} all-gather(f32[4096]{0:T(1024)S(1)} %get-tuple-element.543), channel_id=11, replica_groups=mesh['tm'=4,'space'=2,'hyp'=4] {'tm'}, dimensions={0}, use_global_device_ids=true | all-gather | bytes 81920 | tf_op jit(solution)/shard_map/all_gather | solution.py:30
  304.8 0.4 fusion.12
  305.5 0.7 maximum_bitcast_fusion
  306.3 0.6 constant_dynamic-slice_fusion.16
  306.9 41.7 %all-gather.15.cloned.1.call-done = f32[16,5,4096]{2,1,0:T(8,128)} async-done(((f32[1,5,4096]{2,1,0:T(8,128)}), f32[16,5,4096]{2,1,0:T(8,128)}) %all-gather.15.cloned.1.call-update) | async-done | bytes 1310736 | tf_op jit(solution)/shard_map/all_gather | solution.py:10
  348.6 1.7 reduce_sum.49
  350.3 0.6 slice.37
  351.0 0.6 slice.36
  (342 shorter events, 37.1 us)
Async XLA Ops:
  7.2 341.4 %all-gather.15.cloned.1.call-start = ((), (), s32[]{:S(2)}) async-start(), calls=%async_computation | async-start | bytes 2228224 | tf_op jit(solution)/shard_map/all_gather | solution.py:10
  8.0 10.1 %collective-permute-start = (f32[64]{0:T(128)S(1)}, f32[64]{0:T(128)S(1)}, u32[]{:S(2)}, u32[]{:S(2)}) collective-permute-start(f32[64]{0:T(128)S(1)} %get-tuple-element.865), channel_id=1, source_target_pairs={{0,4},{1,5},{2,6},{3,7},{8,12},{9,13},{10,14},{11,15},{16,20},{17,... | collective-permute-start | bytes 776 | tf_op jit(solution)/shard_map/ppermute | solution.py:18
  11.4 6.7 %collective-permute-start.1 = (f32[64]{0:T(128)S(1)}, f32[64]{0:T(128)S(1)}, u32[]{:S(2)}, u32[]{:S(2)}) collective-permute-start(f32[64]{0:T(128)S(1)} %get-tuple-element.864), channel_id=1, source_target_pairs={{4,0},{5,1},{6,2},{7,3},{12,8},{13,9},{14,10},{15,11},{20,16},{21,... | collective-permute-start | bytes 776 | tf_op jit(solution)/shard_map/ppermute | solution.py:21
  18.2 90.7 %copy-start.3 = (s32[4,4096]{1,0:T(4,128)S(1)}, s32[4,4096]{1,0:T(4,128)}, u32[]{:S(2)}) copy-start(s32[4,4096]{1,0:T(4,128)} %param.26) | copy-start | bytes 196612
  18.2 90.7 %copy-start.4 = (f32[4,4096]{1,0:T(4,128)S(1)}, f32[4,4096]{1,0:T(4,128)}, u32[]{:S(2)}) copy-start(f32[4,4096]{1,0:T(4,128)} %param.25) | copy-start | bytes 196612
  18.3 90.8 %copy-start.5 = (f32[4096]{0:T(1024)S(1)}, f32[4096]{0:T(1024)}, u32[]{:S(2)}) copy-start(f32[4096]{0:T(1024)} %param.24) | copy-start | bytes 49156
  18.3 90.8 %copy-start.6 = (f32[4096]{0:T(1024)S(1)}, f32[4096]{0:T(1024)}, u32[]{:S(2)}) copy-start(f32[4096]{0:T(1024)} %param.22) | copy-start | bytes 49156
  18.3 90.8 %copy-start.7 = (f32[4096]{0:T(1024)S(1)}, f32[4096]{0:T(1024)}, u32[]{:S(2)}) copy-start(f32[4096]{0:T(1024)} %param.23) | copy-start | bytes 49156
  18.3 91.9 %copy-start = (f32[16,4096]{1,0:T(8,128)S(1)}, f32[16,4096]{1,0:T(8,128)}, u32[]{:S(2)}) copy-start(f32[16,4096]{1,0:T(8,128)} %param.29) | copy-start | bytes 786436
  18.3 91.9 %copy-start.1 = (f32[16,4096]{1,0:T(8,128)S(1)}, f32[16,4096]{1,0:T(8,128)}, u32[]{:S(2)}) copy-start(f32[16,4096]{1,0:T(8,128)} %param.27) | copy-start | bytes 786436
  18.3 91.9 %copy-start.2 = (f32[16,4096]{1,0:T(8,128)S(1)}, f32[16,4096]{1,0:T(8,128)}, u32[]{:S(2)}) copy-start(f32[16,4096]{1,0:T(8,128)} %param.28) | copy-start | bytes 786436
Sparse Core Ops, SparseCore 0:
  306.4 42.1 all-gather.14
